TPU v7x, 32 devices: a whole 2x2x4 slice. The times are simulated.
32 devices in a mesh: rep: 8 (over z, core), tp: 4 (over y, x).
Axes of the slice: x: 2, y: 2, z: 4, core: 2. Of those that a mesh axis runs over, the one named last changes fastest.
Arguments:
- partials: bfloat16 [512, 32768], P('rep', 'tp'), may hold values from -6 to 6
- residual: bfloat16 [512, 8192], P('rep', 'tp'), may hold values from -6 to 6
- lower: bfloat16 [512, 8192], P('rep', 'tp'), may hold values from -6 to 6
- middle: bfloat16 [512, 8192], P('rep', 'tp'), may hold values from -6 to 6
- accepted: int32 [256], P('rep'), may hold values from 0 to 63
- fc_weight: bfloat16 [3, 8192, 8192], P(None, 'rep', 'tp')
- norm_gain: float32 [8192], P('tp'), may hold values from 0.1 to 1.9
- grad_normed: bfloat16 [256, 8192], P('rep', 'tp')
Outputs:
- normed: bfloat16 [256, 8192], P('rep', 'tp')
- grad_fc: bfloat16 [3, 8192, 8192], P(None, 'rep', 'tp')
All inputs are finite; a program needn't handle non-finite values.
Results may differ from a plain program's by a relative error of at most 0.017.
Values may be sent and summed in bfloat16 or wider, within the bound.
No kernel may reach another device: no remote copies, remote signals or barrier semaphores. Data moves between devices by JAX's collectives and lax.ppermute only.
A program may use at most 64 MiB of HBM per device.

v0:
```python
import jax
import jax.numpy as jnp
from jax import lax
from jax.sharding import PartitionSpec as P

D = 8192
EPSILON = 1e-06


def xor_exchange(chunk_of, axis, size):
    for k in range(1, size):
        perm = [(i, i ^ k) for i in range(size)]
        yield lax.ppermute(chunk_of(k), axis, perm)


def body(partials, residual, lower, middle, accepted, fc_weight, norm_gain, grad_normed):
    rep_count = lax.axis_size("rep")
    tp_count = lax.axis_size("tp")
    rep_index = lax.axis_index("rep")
    tp_index = lax.axis_index("tp")
    rows = accepted.shape[0]
    tp_width = residual.shape[1]
    picked = jnp.take(partials, accepted, axis=0).reshape(rows, tp_count, tp_width)
    summed = jnp.take(picked, tp_index, axis=1).astype(jnp.float32)
    for got in xor_exchange(lambda k: jnp.take(picked, tp_index ^ k, axis=1), "tp", tp_count):
        summed = summed + got.astype(jnp.float32)
    upper_rows = (jnp.take(residual, accepted, axis=0).astype(jnp.float32) + summed).astype(
        jnp.bfloat16
    )
    local_rows = jnp.stack(
        [jnp.take(lower, accepted, axis=0), jnp.take(middle, accepted, axis=0), upper_rows], axis=1
    )
    slab_width = D // rep_count
    group = rep_count // tp_count
    slabs = local_rows.reshape(rows, 3, group, slab_width)
    received = []
    for c in range(group):
        perm = []
        for r in range(rep_count):
            for t in range(tp_count):
                s = group * t + (r - c) % group
                perm.append((r * tp_count + t, s * tp_count + r // group))
        block = jnp.take(slabs, (rep_index - c) % group, axis=2)
        received.append(lax.ppermute(block, ("rep", "tp"), perm))
    stacked = jnp.stack(received, axis=0)
    order = (jnp.arange(group, dtype=jnp.int32) - rep_index) % group
    mine = jnp.take(stacked, order, axis=0).reshape(group * rows, 3, slab_width)
    features = lax.all_gather(mine, "tp", axis=0, tiled=True)
    total_rows = features.shape[0]
    feature_flat = features.reshape(total_rows, 3 * slab_width)
    fc_block = fc_weight.reshape(3 * slab_width, fc_weight.shape[2])
    hidden = lax.psum_scatter(
        jnp.dot(feature_flat, fc_block, preferred_element_type=jnp.float32),
        "rep",
        scatter_dimension=0,
        tiled=True,
    )
    squares = lax.psum(jnp.sum(hidden * hidden, axis=1), "tp")
    inv_rms = lax.rsqrt(squares / D + EPSILON)
    normed = (hidden * inv_rms[:, None] * norm_gain).astype(jnp.bfloat16)
    scaled = grad_normed.astype(jnp.float32) * norm_gain
    inner_sum = lax.psum(jnp.sum(scaled * hidden, axis=1), "tp")
    hidden_grads = (
        inv_rms[:, None] * scaled - hidden * (inv_rms**3 * inner_sum / D)[:, None]
    ).astype(jnp.bfloat16)
    hidden_grads_all = lax.all_gather(hidden_grads, "rep", axis=0, tiled=True)
    grad_fc = lax.dot_general(
        feature_flat, hidden_grads_all, (((0,), (0,)), ((), ())), preferred_element_type=jnp.float32
    )
    grad_fc = grad_fc.reshape(fc_weight.shape).astype(jnp.bfloat16)
    return (normed, grad_fc)


def solution(mesh):
    in_specs = (
        P("rep", "tp"),
        P("rep", "tp"),
        P("rep", "tp"),
        P("rep", "tp"),
        P("rep"),
        P(None, "rep", "tp"),
        P("tp"),
        P("rep", "tp"),
    )
    out_specs = (P("rep", "tp"), P(None, "rep", "tp"))
    return jax.shard_map(body, mesh=mesh, in_specs=in_specs, out_specs=out_specs, check_vma=False)
```

profile of v0, /device:TPU:0, one launch (start us, length us, event | category | flops | bytes accessed | tf_op | source)
XLA Modules:
  0.0 174.8 jit_solution(10353855674359227189)
XLA Ops:
  7.3 0.7 compare_and_fusion
  8.0 0.7 compare_select_fusion
  8.7 0.9 gather_fusion
  9.6 0.1 bitcast_select_fusion
  9.8 3.0 %collective-permute-start = (bf16[32,2048]{1,0:T(8,128)(2,1)S(1)}, bf16[32,2048]{1,0:T(8,128)(2,1)S(1)}, u32[]{:S(2)}, u32[]{:S(2)}) collective-permute-start(bf16[32,2048]{1,0:T(8,128)(2,1)S(1)} %get-tuple-element.31), channel_id=1, source_target_pairs={{0,1},{1,0},{2,3},{3,2},{4,5},{5,4},{6,7},{7,6},{8,9},{9,8},{10,11... | collective-permute-start | bytes 393224 | tf_op jit(solution)/shard_map/ppermute | solution.py:13
  12.8 1.5 collective-permute-start.2
  14.5 0.6 gather_fusion.4
  15.2 0.7 gather_fusion.3
  15.8 0.7 gather_fusion.2
  16.9 3.6 %collective-permute-done.2 = bf16[32,2048]{1,0:T(8,128)(2,1)S(1)} collective-permute-done((bf16[32,2048]{1,0:T(8,128)(2,1)S(1)}, bf16[32,2048]{1,0:T(8,128)(2,1)S(1)}, u32[]{:S(2)}, u32[]{:S(2)}) %collective-permute-start.2) | collective-permute-done | bytes 131104 | tf_op jit(solution)/shard_map/ppermute | solution.py:13
  20.4 1.4 collective-permute-done.1
  22.1 0.7 collective-permute-start.3
  22.9 1.4 collective-permute-done.4
  24.3 0.6 gather_fusion.1
  24.9 0.9 bitcast_select_fusion.1
  25.8 57.1 %all-gather.3.cloned.1.call-done = bf16[256,3,1024]{2,0,1:T(8,128)(2,1)} async-done(((bf16[64,3,1024]{2,0,1:T(8,128)(2,1)}), bf16[256,3,1024]{2,0,1:T(8,128)(2,1)}) %all-gather.3.cloned.1.call-update) | async-done | bytes 1572880 | tf_op jit(solution)/shard_map/all_gather | solution.py:48
  82.9 9.8 %convolution_bitcast_fusion = f32[256,2048]{1,0:T(8,128)} fusion(bf16[256,3,1024]{2,0,1:T(8,128)(2,1)} %all-gather.3.cloned.1.call-done, bf16[3,1024,2048]{2,1,0:T(8,128)(2,1)} %param.19), kind=kOutput, calls=%fused_computation.6 | convolution fusion | flops 3221225472 | bytes 16252928 | tf_op jit(solution)/shard_map/dot_general | solution.py:53
  92.8 36.2 %reduce-scatter.2.cloned.1.call-done = f32[32,2048]{1,0:T(8,128)} async-done(((f32[256,2048]{1,0:T(8,128)}), f32[32,2048]{1,0:T(8,128)}) %reduce-scatter.2.cloned.1.call-update) | async-done | bytes 262160 | tf_op jit(solution)/shard_map/reduce_scatter | solution.py:52
  129.0 1.1 multiply_reduce_fusion
  130.1 9.8 %all-reduce = (f32[32]{0:T(128)S(1)}, f32[32]{0:T(128)S(1)}) all-reduce(f32[32]{0:T(128)S(1)} %get-tuple-element.28, f32[32]{0:T(128)S(1)} %get-tuple-element.27), channel_id=1, replica_groups=mesh['rep'=8,'tp'=4] {'tp'}, use_global_device_ids=true, to_apply=%region_2.6 | all-reduce | flops 64 | bytes 512 | tf_op jit(solution)/shard_map/psum | solution.py:58
  139.9 1.8 %subtract_convert_fusion = (bf16[32,2048]{1,0:T(8,128)(2,1)}, bf16[32,2048]{1,0:T(8,128)(2,1)}) fusion(f32[32,2048]{1,0:T(8,128)} %reduce-scatter.2.cloned.1.call-done, bf16[32,2048]{1,0:T(8,128)(2,1)S(1)} %copy-done.4, f32[32]{0:T(128)S(1)} %get-tuple-element.38, f32[2048]{0:T(1024)S(1)} %copy-done.5, f32[32]{0:T(128)S(1)} %get-tuple-element.39), kind=kLoop, calls=%fused_computation.12 | loop fusion | flops 589824 | bytes 663808 | tf_op jit(solution)/shard_map/convert_element_type | solution.py:65
  141.7 1.7 copy.16
  143.4 17.0 %all-gather.5.cloned.1.call-done = bf16[256,2048]{1,0:T(8,128)(2,1)} async-done(((bf16[32,2048]{1,0:T(8,128)(2,1)}), bf16[256,2048]{1,0:T(8,128)(2,1)}) %all-gather.5.cloned.1.call-update) | async-done | bytes 1048592 | tf_op jit(solution)/shard_map/all_gather | solution.py:66
  160.5 7.8 %convolution_convert_fusion = bf16[3,1024,2048]{2,1,0:T(8,128)(2,1)} fusion(bf16[256,3,1024]{0,2,1:T(8,128)(2,1)S(1)} %copy.16, bf16[256,2048]{1,0:T(8,128)(2,1)} %all-gather.5.cloned.1.call-done), kind=kOutput, calls=%fused_computation.5 | convolution fusion | flops 3227516928 | bytes 15204352 | tf_op jit(solution)/shard_map/dot_general | solution.py:67
  (41 shorter events, 1.2 us)
Async XLA Ops:
  7.2 1.5 copy-start
  7.2 75.8 %all-gather.3.cloned.1.call-start = ((), (), s32[]{:S(2)}) async-start(), calls=%async_computation.1 | async-start | bytes 1966080 | tf_op jit(solution)/shard_map/all_gather | solution.py:48
  9.5 5.0 %copy-start.1 = (bf16[64,2048]{1,0:T(8,128)(2,1)S(1)}, bf16[64,2048]{1,0:T(8,128)(2,1)}, u32[]{:S(2)}) copy-start(bf16[64,2048]{1,0:T(8,128)(2,1)} %param.15) | copy-start | bytes 786436
  9.6 5.6 %copy-start.2 = (bf16[64,2048]{1,0:T(8,128)(2,1)S(1)}, bf16[64,2048]{1,0:T(8,128)(2,1)}, u32[]{:S(2)}) copy-start(bf16[64,2048]{1,0:T(8,128)(2,1)} %param.17) | copy-start | bytes 786436
  9.6 6.3 %copy-start.3 = (bf16[64,2048]{1,0:T(8,128)(2,1)S(1)}, bf16[64,2048]{1,0:T(8,128)(2,1)}, u32[]{:S(2)}) copy-start(bf16[64,2048]{1,0:T(8,128)(2,1)} %param.16) | copy-start | bytes 786436
  9.8 7.1 %collective-permute-start = (bf16[32,2048]{1,0:T(8,128)(2,1)S(1)}, bf16[32,2048]{1,0:T(8,128)(2,1)S(1)}, u32[]{:S(2)}, u32[]{:S(2)}) collective-permute-start(bf16[32,2048]{1,0:T(8,128)(2,1)S(1)} %get-tuple-element.31), channel_id=1, source_target_pairs={{0,1},{1,0},{2,3},{3,2},{4,5},{5,4},{6,7},{7,6},{8,9},{9,8},{10,11... | collective-permute-start | bytes 393224 | tf_op jit(solution)/shard_map/ppermute | solution.py:13
  12.8 7.6 %collective-permute-start.2 = (bf16[32,2048]{1,0:T(8,128)(2,1)S(1)}, bf16[32,2048]{1,0:T(8,128)(2,1)S(1)}, u32[]{:S(2)}, u32[]{:S(2)}) collective-permute-start(bf16[32,2048]{1,0:T(8,128)(2,1)S(1)} %get-tuple-element.32), channel_id=1, source_target_pairs={{0,3},{1,2},{2,1},{3,0},{4,7},{5,6},{6,5},{7,4},{8,11},{9,10},{10,... | collective-permute-start | bytes 393224 | tf_op jit(solution)/shard_map/ppermute | solution.py:13
  14.3 7.5 %collective-permute-start.1 = (bf16[32,2048]{1,0:T(8,128)(2,1)S(1)}, bf16[32,2048]{1,0:T(8,128)(2,1)S(1)}, u32[]{:S(2)}, u32[]{:S(2)}) collective-permute-start(bf16[32,2048]{1,0:T(8,128)(2,1)S(1)} %get-tuple-element.33), channel_id=1, source_target_pairs={{0,2},{1,3},{2,0},{3,1},{4,6},{5,7},{6,4},{7,5},{8,10},{9,11},{10,... | collective-permute-start | bytes 393224 | tf_op jit(solution)/shard_map/ppermute | solution.py:13
  22.1 0.8 collective-permute-start.3
  22.7 1.5 collective-permute-start.4
  25.8 103.2 %reduce-scatter.2.cloned.1.call-start = ((), (), s32[]{:S(2)}) async-start(), calls=%async_computation.2 | async-start | bytes 2359296 | tf_op jit(solution)/shard_map/reduce_scatter | solution.py:52
  92.7 36.3 %copy-start.4 = (bf16[32,2048]{1,0:T(8,128)(2,1)S(1)}, bf16[32,2048]{1,0:T(8,128)(2,1)}, u32[]{:S(2)}) copy-start(bf16[32,2048]{1,0:T(8,128)(2,1)} %param.21) | copy-start | bytes 393220
  92.7 36.3 %copy-start.5 = (f32[2048]{0:T(1024)S(1)}, f32[2048]{0:T(1024)}, u32[]{:S(2)}) copy-start(f32[2048]{0:T(1024)} %param.20) | copy-start | bytes 24580
  92.8 67.7 %all-gather.5.cloned.1.call-start = ((), (), s32[]{:S(2)}) async-start(), calls=%async_computation.3 | async-start | bytes 1179648 | tf_op jit(solution)/shard_map/all_gather | solution.py:66
Sparse Core Ops, SparseCore 0:
  25.9 56.9 all-gather.2
  92.9 36.0 reduce-scatter.1
  141.8 18.5 all-gather.4
where the time goes:
time: 175 us
  waiting for transfers between devices  117 us (67%)
  matrix products  17.6 us (10%)
  between operations  14 us (8%)
  blocking collectives  9.79 us (6%)
  local copies, waits for them, and re-layouts  5.65 us (3%)
  other arithmetic  5.65 us (3%)
  starting transfers between devices  5.44 us (3%)
    all_gather x1, waiting for transfers between devices, body(): features = lax.all_gather(mine, 'tp', axis=0, tiled=True)  57.1 us
    reduce_scatter x1, waiting for transfers between devices, body(): lax.psum_scatter(jnp.dot(feature_flat, fc_block, preferred_element_type=j...  36.2 us
    all_gather x1, waiting for transfers between devices, body(): hidden_grads_all = lax.all_gather(hidden_grads, 'rep', axis=0, tiled=True)  17 us
    psum x1, blocking collectives, body(): squares = lax.psum(jnp.sum(hidden * hidden, axis=1), 'tp')  9.79 us
    dot_general x1, matrix products, body(): jnp.dot(feature_flat, fc_block, preferred_element_type=jnp.float32)  9.79 us
    dot_general x1, matrix products, body(): lax.dot_general(feature_flat, hidden_grads_all, (((0,), (0,)), ((), ())),...  7.8 us
    ppermute x3, waiting for transfers between devices, xor_exchange(): yield lax.ppermute(chunk_of(k), axis, perm)  4.92 us
    ppermute x3, starting transfers between devices, xor_exchange(): yield lax.ppermute(chunk_of(k), axis, perm)  4.57 us
  transfers between devices with their start and end apart: 8, of which 6 were waited for; matrix products, arithmetic and copies ran while one was open for 2% of the time, Pallas kernels for 0%

commit v1 on v0

--- a/solution.py
+++ b/solution.py
@@ -5,6 +5,22 @@
 
 D = 8192
 EPSILON = 1e-06
+
+
+def perform_the_ports(local_x, on_dim):
+    main = jax.lax.psum(1, axis_name="rep")
+    raw_out = jax.lax.axis_index("rep")
+    f_next, formed = (main, raw_out)
+    near, inter = (local_x, 1)
+    while inter < f_next:
+        f_now = jax.lax.ppermute(
+            near, axis_name="rep", perm=[(no, no ^ inter) for no in range(f_next)]
+        )
+        new = jnp.concatenate([near, f_now], on_dim)
+        res = jnp.concatenate([f_now, near], on_dim)
+        near = jnp.where(formed & inter == 0, new, res)
+        inter = 2 * inter
+    return near
 
 
 def xor_exchange(chunk_of, axis, size):
@@ -63,7 +79,7 @@
     hidden_grads = (
         inv_rms[:, None] * scaled - hidden * (inv_rms**3 * inner_sum / D)[:, None]
     ).astype(jnp.bfloat16)
-    hidden_grads_all = lax.all_gather(hidden_grads, "rep", axis=0, tiled=True)
+    hidden_grads_all = perform_the_ports(hidden_grads, 0)
     grad_fc = lax.dot_general(
         feature_flat, hidden_grads_all, (((0,), (0,)), ((), ())), preferred_element_type=jnp.float32
     )

time: 175 us -> 192 us (1.097)
  waiting for transfers between devices: 117 us -> 133 us
    ppermute x0 -> x3, waiting for transfers between devices: none -> 33.3 us  [perform_the_ports(): jax.lax.ppermute(near, axis_name='rep', perm=[(no, no ^ inter) for no in...]
    all_gather x1 -> x0, waiting for transfers between devices: 17 us -> none  [body(): hidden_grads_all = lax.all_gather(hidden_grads, 'rep', axis=0, tiled=True)]
  transfers between devices with their start and end apart: 8 -> 10, of which waited for: 6 -> 8; matrix products, arithmetic and copies ran while one was open for 2% -> 2% of each run, Pallas kernels for 0% -> 0%
where the time goes in v1:
time: 192 us
  waiting for transfers between devices  133 us (69%)
  matrix products  17.6 us (9%)
  between operations  14.3 us (7%)
  blocking collectives  9.79 us (5%)
  other arithmetic  5.74 us (3%)
  local copies, waits for them, and re-layouts  5.65 us (3%)
  starting transfers between devices  5.54 us (3%)
    all_gather x1, waiting for transfers between devices, body(): features = lax.all_gather(mine, 'tp', axis=0, tiled=True)  57.1 us
    reduce_scatter x1, waiting for transfers between devices, body(): lax.psum_scatter(jnp.dot(feature_flat, fc_block, preferred_element_type=j...  36.2 us
    ppermute x3, waiting for transfers between devices, perform_the_ports(): jax.lax.ppermute(near, axis_name='rep', perm=[(no, no ^ inter) for no in...  33.3 us
    psum x1, blocking collectives, body(): squares = lax.psum(jnp.sum(hidden * hidden, axis=1), 'tp')  9.79 us
    dot_general x1, matrix products, body(): jnp.dot(feature_flat, fc_block, preferred_element_type=jnp.float32)  9.79 us
    dot_general x1, matrix products, body(): lax.dot_general(feature_flat, hidden_grads_all, (((0,), (0,)), ((), ())),...  7.81 us
    ppermute x3, waiting for transfers between devices, xor_exchange(): yield lax.ppermute(chunk_of(k), axis, perm)  4.92 us
    ppermute x3, starting transfers between devices, xor_exchange(): yield lax.ppermute(chunk_of(k), axis, perm)  4.57 us
  transfers between devices with their start and end apart: 10, of which 8 were waited for; matrix products, arithmetic and copies ran while one was open for 2% of the time, Pallas kernels for 0%

profile of v1, /device:TPU:0, one launch (start us, length us, event | category | flops | bytes accessed | tf_op | source)
XLA Modules:
  0.0 191.6 jit_solution(13175598719970347380)
XLA Ops:
  7.3 0.7 compare_and_fusion
  8.0 0.7 compare_select_fusion
  8.7 0.9 gather_fusion
  9.8 3.0 %collective-permute-start = (bf16[32,2048]{1,0:T(8,128)(2,1)S(1)}, bf16[32,2048]{1,0:T(8,128)(2,1)S(1)}, u32[]{:S(2)}, u32[]{:S(2)}) collective-permute-start(bf16[32,2048]{1,0:T(8,128)(2,1)S(1)} %get-tuple-element.31), channel_id=1, source_target_pairs={{0,1},{1,0},{2,3},{3,2},{4,5},{5,4},{6,7},{7,6},{8,9},{9,8},{10,11... | collective-permute-start | bytes 393224 | tf_op jit(solution)/shard_map/ppermute | solution.py:29
  12.8 1.5 collective-permute-start.2
  14.5 0.6 gather_fusion.4
  15.2 0.7 gather_fusion.3
  15.8 0.7 gather_fusion.2
  16.9 3.6 %collective-permute-done.2 = bf16[32,2048]{1,0:T(8,128)(2,1)S(1)} collective-permute-done((bf16[32,2048]{1,0:T(8,128)(2,1)S(1)}, bf16[32,2048]{1,0:T(8,128)(2,1)S(1)}, u32[]{:S(2)}, u32[]{:S(2)}) %collective-permute-start.2) | collective-permute-done | bytes 131104 | tf_op jit(solution)/shard_map/ppermute | solution.py:29
  20.4 1.4 collective-permute-done.1
  22.1 0.7 collective-permute-start.3
  22.9 1.4 collective-permute-done.4
  24.9 0.9 bitcast_select_fusion.1
  25.8 57.1 %all-gather.2.cloned.1.call-done = bf16[256,3,1024]{2,0,1:T(8,128)(2,1)} async-done(((bf16[64,3,1024]{2,0,1:T(8,128)(2,1)}), bf16[256,3,1024]{2,0,1:T(8,128)(2,1)}) %all-gather.2.cloned.1.call-update) | async-done | bytes 1572880 | tf_op jit(solution)/shard_map/all_gather | solution.py:64
  82.9 9.8 %convolution_bitcast_fusion = f32[256,2048]{1,0:T(8,128)} fusion(bf16[256,3,1024]{2,0,1:T(8,128)(2,1)} %all-gather.2.cloned.1.call-done, bf16[3,1024,2048]{2,1,0:T(8,128)(2,1)} %param.19), kind=kOutput, calls=%fused_computation.6 | convolution fusion | flops 3221225472 | bytes 16252928 | tf_op jit(solution)/shard_map/dot_general | solution.py:69
  92.8 36.2 %reduce-scatter.2.cloned.1.call-done = f32[32,2048]{1,0:T(8,128)} async-done(((f32[256,2048]{1,0:T(8,128)}), f32[32,2048]{1,0:T(8,128)}) %reduce-scatter.2.cloned.1.call-update) | async-done | bytes 262160 | tf_op jit(solution)/shard_map/reduce_scatter | solution.py:68
  129.0 1.1 multiply_reduce_fusion
  130.1 9.8 %all-reduce = (f32[32]{0:T(128)S(1)}, f32[32]{0:T(128)S(1)}) all-reduce(f32[32]{0:T(128)S(1)} %get-tuple-element.28, f32[32]{0:T(128)S(1)} %get-tuple-element.27), channel_id=1, replica_groups=mesh['rep'=8,'tp'=4] {'tp'}, use_global_device_ids=true, to_apply=%region_2.6 | all-reduce | flops 64 | bytes 512 | tf_op jit(solution)/shard_map/psum | solution.py:74
  139.9 1.7 subtract_convert_fusion
  141.6 1.3 collective-permute-done.5
  143.1 8.3 %collective-permute-done.6 = bf16[64,2048]{1,0:T(8,128)(2,1)S(1)} collective-permute-done((bf16[64,2048]{1,0:T(8,128)(2,1)S(1)}, bf16[64,2048]{1,0:T(8,128)(2,1)S(1)}, u32[]{:S(2)}, u32[]{:S(2)}) %collective-permute-start.6) | collective-permute-done | bytes 262176 | tf_op jit(solution)/shard_map/ppermute | solution.py:16
  151.7 1.7 copy.16
  153.4 23.6 %collective-permute-done.7 = bf16[128,2048]{1,0:T(8,128)(2,1)} collective-permute-done((bf16[128,2048]{1,0:T(8,128)(2,1)S(1)}, bf16[128,2048]{1,0:T(8,128)(2,1)}, u32[]{:S(2)}, u32[]{:S(2)}) %collective-permute-start.7) | collective-permute-done | bytes 524320 | tf_op jit(solution)/shard_map/ppermute | solution.py:16
  177.0 7.8 %convolution_convert_fusion = bf16[3,1024,2048]{2,1,0:T(8,128)(2,1)} fusion(bf16[256,3,1024]{0,2,1:T(8,128)(2,1)S(1)} %copy.16, bf16[128,2048]{1,0:T(8,128)(2,1)} %collective-permute-done.7, bf16[128,2048]{1,0:T(8,128)(2,1)S(1)} %maximum_select_fusion.1, pred[]{:T(512)S(6)} %eq.14), kind=kOutput, calls=%fused_computation.5 | convolution fusion | flops 3232235520 | bytes 15204353 | tf_op jit(solution)/shard_map/dot_general | solution.py:83
  (46 shorter events, 2.2 us)
Async XLA Ops:
  7.2 1.5 copy-start
  7.2 75.8 %all-gather.2.cloned.1.call-start = ((), (), s32[]{:S(2)}) async-start(), calls=%async_computation.1 | async-start | bytes 1966080 | tf_op jit(solution)/shard_map/all_gather | solution.py:64
  9.5 5.0 %copy-start.1 = (bf16[64,2048]{1,0:T(8,128)(2,1)S(1)}, bf16[64,2048]{1,0:T(8,128)(2,1)}, u32[]{:S(2)}) copy-start(bf16[64,2048]{1,0:T(8,128)(2,1)} %param.15) | copy-start | bytes 786436
  9.6 5.6 %copy-start.2 = (bf16[64,2048]{1,0:T(8,128)(2,1)S(1)}, bf16[64,2048]{1,0:T(8,128)(2,1)}, u32[]{:S(2)}) copy-start(bf16[64,2048]{1,0:T(8,128)(2,1)} %param.17) | copy-start | bytes 786436
  9.6 6.3 %copy-start.3 = (bf16[64,2048]{1,0:T(8,128)(2,1)S(1)}, bf16[64,2048]{1,0:T(8,128)(2,1)}, u32[]{:S(2)}) copy-start(bf16[64,2048]{1,0:T(8,128)(2,1)} %param.16) | copy-start | bytes 786436
  9.8 7.1 %collective-permute-start = (bf16[32,2048]{1,0:T(8,128)(2,1)S(1)}, bf16[32,2048]{1,0:T(8,128)(2,1)S(1)}, u32[]{:S(2)}, u32[]{:S(2)}) collective-permute-start(bf16[32,2048]{1,0:T(8,128)(2,1)S(1)} %get-tuple-element.31), channel_id=1, source_target_pairs={{0,1},{1,0},{2,3},{3,2},{4,5},{5,4},{6,7},{7,6},{8,9},{9,8},{10,11... | collective-permute-start | bytes 393224 | tf_op jit(solution)/shard_map/ppermute | solution.py:29
  12.8 7.6 %collective-permute-start.2 = (bf16[32,2048]{1,0:T(8,128)(2,1)S(1)}, bf16[32,2048]{1,0:T(8,128)(2,1)S(1)}, u32[]{:S(2)}, u32[]{:S(2)}) collective-permute-start(bf16[32,2048]{1,0:T(8,128)(2,1)S(1)} %get-tuple-element.32), channel_id=1, source_target_pairs={{0,3},{1,2},{2,1},{3,0},{4,7},{5,6},{6,5},{7,4},{8,11},{9,10},{10,... | collective-permute-start | bytes 393224 | tf_op jit(solution)/shard_map/ppermute | solution.py:29
  14.3 7.5 %collective-permute-start.1 = (bf16[32,2048]{1,0:T(8,128)(2,1)S(1)}, bf16[32,2048]{1,0:T(8,128)(2,1)S(1)}, u32[]{:S(2)}, u32[]{:S(2)}) collective-permute-start(bf16[32,2048]{1,0:T(8,128)(2,1)S(1)} %get-tuple-element.33), channel_id=1, source_target_pairs={{0,2},{1,3},{2,0},{3,1},{4,6},{5,7},{6,4},{7,5},{8,10},{9,11},{10,... | collective-permute-start | bytes 393224 | tf_op jit(solution)/shard_map/ppermute | solution.py:29
  22.1 0.8 collective-permute-start.3
  22.7 1.5 collective-permute-start.4
  25.8 103.2 %reduce-scatter.2.cloned.1.call-start = ((), (), s32[]{:S(2)}) async-start(), calls=%async_computation.2 | async-start | bytes 2359296 | tf_op jit(solution)/shard_map/reduce_scatter | solution.py:68
  92.7 36.3 %copy-start.4 = (bf16[32,2048]{1,0:T(8,128)(2,1)S(1)}, bf16[32,2048]{1,0:T(8,128)(2,1)}, u32[]{:S(2)}) copy-start(bf16[32,2048]{1,0:T(8,128)(2,1)} %param.21) | copy-start | bytes 393220
  92.7 36.3 %copy-start.5 = (f32[2048]{0:T(1024)S(1)}, f32[2048]{0:T(1024)}, u32[]{:S(2)}) copy-start(f32[2048]{0:T(1024)} %param.20) | copy-start | bytes 24580
  141.6 1.3 collective-permute-start.5
  143.0 8.4 %collective-permute-start.6 = (bf16[64,2048]{1,0:T(8,128)(2,1)S(1)}, bf16[64,2048]{1,0:T(8,128)(2,1)S(1)}, u32[]{:S(2)}, u32[]{:S(2)}) collective-permute-start(bf16[64,2048]{1,0:T(8,128)(2,1)S(1)} %maximum_select_fusion.2), channel_id=1, source_target_pairs={{0,8},{4,12},{8,0},{12,4},{16,24},{20,28},{24,16},{28,20},{1,9},{5... | collective-permute-start | bytes 786440 | tf_op jit(solution)/shard_map/ppermute | solution.py:16
  151.6 25.4 %collective-permute-start.7 = (bf16[128,2048]{1,0:T(8,128)(2,1)S(1)}, bf16[128,2048]{1,0:T(8,128)(2,1)}, u32[]{:S(2)}, u32[]{:S(2)}) collective-permute-start(bf16[128,2048]{1,0:T(8,128)(2,1)S(1)} %maximum_select_fusion.1), channel_id=1, source_target_pairs={{0,16},{4,20},{8,24},{12,28},{16,0},{20,4},{24,8},{28,12},{1,17},{... | collective-permute-start | bytes 1572872 | tf_op jit(solution)/shard_map/ppermute | solution.py:16
Sparse Core Ops, SparseCore 0:
  25.9 56.9 all-gather.1
  92.9 36.0 reduce-scatter.1
